TPU v7x, 32 devices: a whole 2x2x4 slice. The times are simulated.
32 devices in a mesh: tm: 8 (over z, core), space: 4 (over y, x).
Axes of the slice: x: 2, y: 2, z: 4, core: 2. Of those that a mesh axis runs over, the one named last changes fastest.
Arguments:
- volumes: float32 [8, 64, 512, 128], P('tm', 'space'), may hold values from -12 to 12
Outputs:
- corrected: float32 [8, 64, 512, 128], P('tm', 'space')
- shifts: float32 [8, 3], P('tm')
All inputs are finite; a program needn't handle non-finite values.
Results may differ from a plain program's by a relative error of at most 0.0003.
Values sent between devices are 32-bit elements; how exact they have to be, the bound alone decides.
No kernel may reach another device: no remote copies, remote signals or barrier semaphores. Data moves between devices by JAX's collectives and lax.ppermute only.
A program may use at most 128 MiB of HBM per device.

v0:
```python
import math

import jax
import jax.numpy as jnp
from jax import lax
from jax.sharding import PartitionSpec as P

X = 512
Y = 128
Z = 64
ITERS = 2


precise = lax.Precision.HIGHEST
sharpness = 256.0
floor_share = 0.05


def dft_tables(length):
    indices = jnp.arange(length, dtype=jnp.int32)
    products = indices[:, None] * indices[None, :] % length
    angles = products.astype(jnp.float32) * (2.0 * math.pi / length)
    return (jnp.cos(angles), jnp.sin(angles))


def signed_freq(indices, length):
    wrapped = jnp.where(indices < length // 2, indices, indices - length)
    return jnp.where(indices == length // 2, 0, wrapped).astype(jnp.float32)


def centred(indices, length):
    return ((indices + length // 2) % length - length // 2).astype(jnp.float32)


def mix_z(table, data):
    return jnp.einsum("kz,vz...->vk...", table, data, precision=precise)


def mix_x(table, data):
    return jnp.einsum("kx,vzx...->vzk...", table, data, precision=precise)


def mix_y(data, table):
    return jnp.dot(data, table, precision=precise)


def forward(volume, tables):
    cos_x, sin_x, cos_y, sin_y, cos_z, sin_z = tables
    real_x = mix_x(cos_x, volume)
    imag_x = -mix_x(sin_x, volume)
    real_y = mix_y(real_x, cos_y) + mix_y(imag_x, sin_y)
    imag_y = mix_y(imag_x, cos_y) - mix_y(real_x, sin_y)
    real_p, imag_p = (
        lax.all_to_all(real_y, "space", split_axis=2, concat_axis=1, tiled=True),
        lax.all_to_all(imag_y, "space", split_axis=2, concat_axis=1, tiled=True),
    )
    real_z = mix_z(cos_z, real_p) + mix_z(sin_z, imag_p)
    imag_z = mix_z(cos_z, imag_p) - mix_z(sin_z, real_p)
    return (real_z, imag_z)


def inverse(spectrum, tables):
    cos_x, sin_x, cos_y, sin_y, cos_z, sin_z = tables
    norming = 1.0 / (X * Y * Z)
    real_in, imag_in = spectrum
    real_z = mix_z(cos_z, real_in) - mix_z(sin_z, imag_in)
    imag_z = mix_z(sin_z, real_in) + mix_z(cos_z, imag_in)
    real_y = mix_y(real_z, cos_y) - mix_y(imag_z, sin_y)
    imag_y = mix_y(real_z, sin_y) + mix_y(imag_z, cos_y)
    real_s, imag_s = (
        lax.all_to_all(real_y, "space", split_axis=1, concat_axis=2, tiled=True),
        lax.all_to_all(imag_y, "space", split_axis=1, concat_axis=2, tiled=True),
    )
    return (mix_x(cos_x, real_s) - mix_x(sin_x, imag_s)) * norming


def split_pairs(spectrum):
    return [(spectrum[0], spectrum[1])]


def join_pairs(pairs):
    return (pairs[0][0], pairs[0][1])


def y_frequencies():
    return [signed_freq(jnp.arange(Y, dtype=jnp.int32), Y)]


def template_sum(spectrum):
    return lax.psum((jnp.sum(spectrum[0], axis=0), jnp.sum(spectrum[1], axis=0)), "tm")


def weight_moments(weights, coords):
    coord_z, coord_x, coord_y = coords
    weight_sum = jnp.sum(weights, axis=(1, 2, 3))
    moment_z = jnp.sum(jnp.sum(weights, axis=(2, 3)) * coord_z[None, :], axis=1)
    moment_x = jnp.sum(jnp.sum(weights, axis=(1, 3)) * coord_x[None, :], axis=1)
    moment_y = jnp.sum(jnp.sum(weights, axis=(1, 2)) * coord_y[None, :], axis=1)
    return (weight_sum, jnp.stack([moment_z, moment_x, moment_y], axis=1))


def centroid(scores, coords):
    local_top = jnp.max(scores, axis=(1, 2, 3))
    top_score = lax.pmax(local_top, "space")
    weights = jnp.exp(scores - top_score[:, None, None, None])
    weight_sum, moments = weight_moments(weights, coords)
    weight_sum, moments = lax.psum((weight_sum, moments), "space")
    return moments / weight_sum[:, None]


def apply_ramp(real_in, imag_in, shifts, freq_z, freq_x, freq_y):
    phases = (
        2.0
        * math.pi
        * (
            freq_z[None, :, None] * (shifts[:, 0] / Z)[:, None, None]
            + freq_x[None, None, :] * (shifts[:, 1] / X)[:, None, None]
        )
    )
    phases = (
        phases[..., None]
        + 2.0 * math.pi * freq_y[None, None, None, :] * (shifts[:, 2] / Y)[:, None, None, None]
    )
    cosine = jnp.cos(phases)
    sine = jnp.sin(phases)
    return (real_in * cosine - imag_in * sine, real_in * sine + imag_in * cosine)


def whiten(spec_re, spec_im, tmpl_re, tmpl_im):
    prod_re = spec_re * tmpl_re + spec_im * tmpl_im
    prod_im = spec_im * tmpl_re - spec_re * tmpl_im
    divisor = jnp.maximum(
        jnp.sqrt(prod_re * prod_re + prod_im * prod_im), floor_share * (X * Y * Z)
    )
    return (prod_re / divisor, prod_im / divisor)


def body(volumes):
    position = lax.axis_index("space")
    slab_depth = volumes.shape[1]
    pencil = X // lax.axis_size("space")
    frames = volumes.shape[0] * lax.axis_size("tm")
    tables = dft_tables(X) + dft_tables(Y) + dft_tables(Z)
    z_index = position * slab_depth + jnp.arange(slab_depth, dtype=jnp.int32)
    x_index = position * pencil + jnp.arange(pencil, dtype=jnp.int32)
    coords = (
        centred(z_index, Z),
        centred(jnp.arange(X, dtype=jnp.int32), X),
        centred(jnp.arange(Y, dtype=jnp.int32), Y),
    )
    freq_z = signed_freq(jnp.arange(Z, dtype=jnp.int32), Z)
    freq_x = signed_freq(x_index, X)
    freq_ys = y_frequencies()
    spectrum = forward(volumes, tables)
    spec_pairs = split_pairs(spectrum)
    shifted = spectrum
    for iteration in range(ITERS):
        summed = template_sum(shifted)
        template = tuple((part[None] / frames for part in summed))
        tmpl_pairs = split_pairs(template)
        white_pairs = [
            whiten(spec_pairs[0][0], spec_pairs[0][1], tmpl_pairs[0][0], tmpl_pairs[0][1])
        ]
        correlation = inverse(join_pairs(white_pairs), tables)
        shifts = centroid(sharpness * correlation, coords)
        ramped = [
            apply_ramp(spec_pairs[0][0], spec_pairs[0][1], shifts, freq_z, freq_x, freq_ys[0])
        ]
        shifted = join_pairs(ramped)
    corrected = inverse(shifted, tables)
    return (corrected, shifts)


def solution(mesh):
    in_specs = (P("tm", "space", None, None),)
    out_specs = (P("tm", "space", None, None), P("tm", None))
    return jax.shard_map(body, mesh=mesh, in_specs=in_specs, out_specs=out_specs, check_vma=False)
```

profile of v0, /device:TPU:0, one launch (start us, length us, event | category | flops | bytes accessed | tf_op | source)
XLA Modules:
  0.0 1235.6 jit_solution(4220639546576311592)
XLA Ops:
  7.2 13.2 %fusion.46 = f32[512,16,128]{2,0,1:T(8,128)S(1)} fusion(f32[1,16,512,128]{3,2,1,0:T(8,128)} %param.1), kind=kOutput, calls=%fused_computation.58 | convolution fusion | flops 6446120960 | bytes 8388608 | tf_op jit(solution)/shard_map/kx,vzx...->vzk.../dot_general | solution.py:40
  20.4 11.1 fusion.44
  63.7 34.3 %all-to-all-done = f32[1,16,512,128]{3,1,0,2:T(8,128)} async-done(((f32[1,16,512,128]{3,1,0,2:T(8,128)}), f32[1,16,512,128]{3,1,0,2:T(8,128)}, u32[]{:S(2)}, u32[]{:S(2)}) %all-to-all-start) | async-done | bytes 4194336 | tf_op jit(solution)/shard_map/all_to_all | solution.py:54
  113.4 36.6 %all-to-all-done.1 = f32[1,16,512,128]{3,1,0,2:T(8,128)} async-done(((f32[1,16,512,128]{3,1,0,2:T(8,128)}), f32[1,16,512,128]{3,1,0,2:T(8,128)}, u32[]{:S(2)}, u32[]{:S(2)}) %all-to-all-start.1) | async-done | bytes 4194336 | tf_op jit(solution)/shard_map/all_to_all | solution.py:55
  168.3 176.1 %all-reduce.9.cloned.1.call-done = (f32[64,128,128]{2,0,1:T(8,128)}, f32[64,128,128]{2,0,1:T(8,128)}) async-done(((f32[64,128,128]{2,0,1:T(8,128)}, f32[64,128,128]{2,0,1:T(8,128)}), (f32[64,128,128]{2,0,1:T(8,128)}, f32[64,128,128]{2,0,1:T(8,128)})) %all-reduce.9.cloned.1.call-update) | async-done | bytes 8388624 | tf_op jit(solution)/shard_map/psum | solution.py:90
  344.4 10.4 fusion.34
  402.8 8.8 fusion.70
  419.8 30.4 %all-to-all-done.3 = f32[1,64,128,128]{3,2,0,1:T(8,128)} async-done(((f32[1,64,128,128]{3,2,0,1:T(8,128)}), f32[1,64,128,128]{3,2,0,1:T(8,128)}, u32[]{:S(2)}, u32[]{:S(2)}) %all-to-all-start.3) | async-done | bytes 4194336 | tf_op jit(solution)/shard_map/all_to_all | solution.py:72
  465.8 36.2 %all-to-all-done.2 = f32[1,64,128,128]{3,2,0,1:T(8,128)} async-done(((f32[1,64,128,128]{3,2,0,1:T(8,128)}), f32[1,64,128,128]{3,2,0,1:T(8,128)}, u32[]{:S(2)}, u32[]{:S(2)}) %all-to-all-start.2) | async-done | bytes 4194336 | tf_op jit(solution)/shard_map/all_to_all | solution.py:71
  512.9 12.9 %fusion.121 = f32[16,128,512]{2,1,0:T(8,128)S(1)} fusion(f32[16,512,128]{1,2,0:T(8,128)} %reshape.463), kind=kOutput, calls=%fused_computation.135 | convolution fusion | flops 6446120960 | bytes 8388608 | tf_op jit(solution)/shard_map/kx,vzx...->vzk.../dot_general | solution.py:40
  525.9 13.1 %fusion.407 = (f32[]{:T(128)}, f32[16,128,512]{2,1,0:T(8,128)}) fusion(f32[16,128,512]{2,1,0:T(8,128)S(1)} %fusion.121, f32[16,512,128]{1,2,0:T(8,128)S(1)} %copy-done.17), kind=kOutput, calls=%fused_computation.410 | convolution fusion | flops 6449266688 | bytes 12582916 | tf_op jit(solution)/shard_map/kx,vzx...->vzk.../dot_general | solution.py:40
  539.0 9.5 pmax.14
  557.7 9.5 all-reduce.3
  570.5 19.2 %fusion.13 = (f32[64,128,128]{2,0,1:T(8,128)}, f32[64,128,128]{2,0,1:T(8,128)}) fusion(f32[128,128,64]{1,2,0:T(8,128)} %convolution_subtract_fusion, f32[128,128,64]{1,2,0:T(8,128)} %convolution_add_fusion, f32[128]{0:T(128)S(1)} %broadcast_multiply_fusion.3, f32[64,128]{0,1:T(8,128)S(1)} %add_multiply_fusion.1), kind=kLoop, calls=%fused_computation.17 | loop fusion | flops 7340032 | bytes 16810496 | tf_op jit(solution)/shard_map/reduce_sum | solution.py:90
  589.7 175.1 %all-reduce.7.cloned.1.call-done = (f32[64,128,128]{2,0,1:T(8,128)}, f32[64,128,128]{2,0,1:T(8,128)}) async-done(((f32[64,128,128]{2,0,1:T(8,128)}, f32[64,128,128]{2,0,1:T(8,128)}), (f32[64,128,128]{2,0,1:T(8,128)}, f32[64,128,128]{2,0,1:T(8,128)})) %all-reduce.7.cloned.1.call-update) | async-done | bytes 8388624 | tf_op jit(solution)/shard_map/psum | solution.py:90
  764.8 10.4 fusion.24
  823.2 8.8 fusion.62
  840.2 30.2 %all-to-all-done.5 = f32[1,64,128,128]{3,2,0,1:T(8,128)} async-done(((f32[1,64,128,128]{3,2,0,1:T(8,128)}), f32[1,64,128,128]{3,2,0,1:T(8,128)}, u32[]{:S(2)}, u32[]{:S(2)}) %all-to-all-start.5) | async-done | bytes 4194336 | tf_op jit(solution)/shard_map/all_to_all | solution.py:72
  886.0 36.3 %all-to-all-done.4 = f32[1,64,128,128]{3,2,0,1:T(8,128)} async-done(((f32[1,64,128,128]{3,2,0,1:T(8,128)}), f32[1,64,128,128]{3,2,0,1:T(8,128)}, u32[]{:S(2)}, u32[]{:S(2)}) %all-to-all-start.4) | async-done | bytes 4194336 | tf_op jit(solution)/shard_map/all_to_all | solution.py:71
  933.2 12.9 %fusion.119 = f32[16,128,512]{2,1,0:T(8,128)S(1)} fusion(f32[16,512,128]{1,2,0:T(8,128)} %reshape.469), kind=kOutput, calls=%fused_computation.133 | convolution fusion | flops 6446120960 | bytes 8388608 | tf_op jit(solution)/shard_map/kx,vzx...->vzk.../dot_general | solution.py:40
  946.1 13.1 %fusion.408 = (f32[]{:T(128)}, f32[16,128,512]{2,1,0:T(8,128)}) fusion(f32[16,128,512]{2,1,0:T(8,128)S(1)} %fusion.119, f32[16,512,128]{1,2,0:T(8,128)S(1)} %copy-done.18), kind=kOutput, calls=%fused_computation.411 | convolution fusion | flops 6449266688 | bytes 12582916 | tf_op jit(solution)/shard_map/kx,vzx...->vzk.../dot_general | solution.py:40
  959.2 9.5 pmax.15
  977.9 9.5 all-reduce.2
  990.8 21.9 %fusion.141 = f32[128,128,64]{1,2,0:T(8,128)S(1)} fusion(f32[128,128,64]{1,2,0:T(8,128)} %convolution_subtract_fusion, f32[128,128,64]{1,2,0:T(8,128)} %convolution_add_fusion, f32[128]{0:T(128)S(1)} %broadcast_multiply_fusion, f32[64,128]{0,1:T(8,128)S(1)} %add_multiply_fusion), kind=kOutput, calls=%fused_computation.144 | convolution fusion | flops 809558016 | bytes 12616192 | tf_op jit(solution)/shard_map/kz,vz...->vk.../dot_general | solution.py:36
  1012.8 19.8 %fusion.139 = f32[128,128,64]{1,2,0:T(8,128)S(1)} fusion(f32[128,128,64]{1,2,0:T(8,128)S(1)} %copy-done.1, f32[128,128,64]{1,2,0:T(8,128)S(1)} %copy-done, f32[128]{0:T(128)S(1)} %broadcast_multiply_fusion, f32[64,128]{0,1:T(8,128)S(1)} %add_multiply_fusion), kind=kOutput, calls=%fused_computation.143 | convolution fusion | flops 809558016 | bytes 12616192 | tf_op jit(solution)/shard_map/kz,vz...->vk.../dot_general | solution.py:36
  1032.6 19.6 %subtract_bitcast_fusion.1 = f32[64,128,128]{2,0,1:T(8,128)S(1)} fusion(f32[128,128,64]{1,2,0:T(8,128)S(1)} %fusion.141, f32[128,128,64]{1,2,0:T(8,128)S(1)} %copy-done.1, f32[128,128,64]{1,2,0:T(8,128)S(1)} %copy-done, f32[128]{0:T(128)S(1)} %broadcast_multiply_fusion, f32[64,128]{0,1:T(8,128)S(1)} %add_multiply_fusion), kind=kOutput, calls=%fused_computation.64 | convolution fusion | flops 810606592 | bytes 16810496 | tf_op jit(solution)/shard_map/kz,vz...->vk.../dot_general | solution.py:36
  1052.2 20.1 %add_bitcast_fusion.1 = f32[64,128,128]{2,0,1:T(8,128)S(1)} fusion(f32[128,128,64]{1,2,0:T(8,128)S(1)} %fusion.139, f32[128,128,64]{1,2,0:T(8,128)S(1)} %copy-done.1, f32[128,128,64]{1,2,0:T(8,128)S(1)} %copy-done, f32[128]{0:T(128)S(1)} %broadcast_multiply_fusion, f32[64,128]{0,1:T(8,128)S(1)} %add_multiply_fusion), kind=kOutput, calls=%fused_computation.63 | convolution fusion | flops 810606592 | bytes 16810496 | tf_op jit(solution)/shard_map/kz,vz...->vk.../dot_general | solution.py:36
  1092.7 8.8 fusion.54
  1109.7 25.1 %all-to-all-done.7 = f32[1,64,128,128]{3,2,0,1:T(8,128)} async-done(((f32[1,64,128,128]{3,2,0,1:T(8,128)}), f32[1,64,128,128]{3,2,0,1:T(8,128)}, u32[]{:S(2)}, u32[]{:S(2)}) %all-to-all-start.7) | async-done | bytes 4194336 | tf_op jit(solution)/shard_map/all_to_all | solution.py:72
  1150.4 36.2 %all-to-all-done.6 = f32[1,64,128,128]{3,2,0,1:T(8,128)} async-done(((f32[1,64,128,128]{3,2,0,1:T(8,128)}), f32[1,64,128,128]{3,2,0,1:T(8,128)}, u32[]{:S(2)}, u32[]{:S(2)}) %all-to-all-start.6) | async-done | bytes 4194336 | tf_op jit(solution)/shard_map/all_to_all | solution.py:71
  1197.5 12.9 %fusion.117 = f32[16,128,512]{2,1,0:T(8,128)S(1)} fusion(f32[16,512,128]{1,2,0:T(8,128)} %reshape.475), kind=kOutput, calls=%fused_computation.131 | convolution fusion | flops 6446120960 | bytes 8388608 | tf_op jit(solution)/shard_map/kx,vzx...->vzk.../dot_general | solution.py:40
  1210.5 12.5 %multiply_bitcast_fusion = f32[1,16,512,128]{2,3,1,0:T(8,128)} fusion(f32[16,128,512]{2,1,0:T(8,128)S(1)} %fusion.117, f32[16,512,128]{1,2,0:T(8,128)S(1)} %copy-done.15), kind=kOutput, calls=%fused_computation.60 | convolution fusion | flops 6448218112 | bytes 12582912 | tf_op jit(solution)/shard_map/kx,vzx...->vzk.../dot_general | solution.py:40
  (124 shorter events, 312.5 us)
Async XLA Ops:
  7.2 13.2 %copy-start.5 = (f32[1,16,512,128]{3,2,1,0:T(8,128)S(1)}, f32[1,16,512,128]{3,2,1,0:T(8,128)}, u32[]{:S(2)}) copy-start(f32[1,16,512,128]{3,2,1,0:T(8,128)} %param.1) | copy-start | bytes 12582916
  20.4 11.1 copy-start.4
  31.5 4.2 copy-start.2
  44.0 54.0 %all-to-all-start = ((f32[1,16,512,128]{3,1,0,2:T(8,128)}), f32[1,16,512,128]{3,1,0,2:T(8,128)}, u32[]{:S(2)}, u32[]{:S(2)}) async-start(f32[1,16,512,128]{3,1,0,2:T(8,128)} %copy.24), calls=%async_computation | async-start | bytes 8388608 | tf_op jit(solution)/shard_map/all_to_all | solution.py:54
  49.4 6.0 copy-start.3
  98.0 52.0 %all-to-all-start.1 = ((f32[1,16,512,128]{3,1,0,2:T(8,128)}), f32[1,16,512,128]{3,1,0,2:T(8,128)}, u32[]{:S(2)}, u32[]{:S(2)}) async-start(f32[1,16,512,128]{3,1,0,2:T(8,128)} %copy.26), calls=%async_computation.1 | async-start | bytes 8388608 | tf_op jit(solution)/shard_map/all_to_all | solution.py:55
  103.0 241.4 %all-reduce.9.cloned.1.call-start = ((), (), s32[]{:S(2)}) async-start(), calls=%async_computation.9 | async-start | bytes 16777216 | tf_op jit(solution)/shard_map/psum | solution.py:90
  157.0 5.4 copy-start.9
  354.8 8.4 copy-start.21
  375.8 13.5 %copy-start.11 = (f32[64,128,128]{2,0,1:T(8,128)}, f32[64,128,128]{2,0,1:T(8,128)S(1)}, u32[]{:S(2)}) copy-start(f32[64,128,128]{2,0,1:T(8,128)S(1)} %subtract_bitcast_fusion.5) | copy-start | bytes 12582916
  382.2 7.1 copy-start.19
  397.5 52.6 %all-to-all-start.3 = ((f32[1,64,128,128]{3,2,0,1:T(8,128)}), f32[1,64,128,128]{3,2,0,1:T(8,128)}, u32[]{:S(2)}, u32[]{:S(2)}) async-start(f32[1,64,128,128]{3,2,0,1:T(8,128)} %add_bitcast_fusion.4), calls=%async_computation.3 | async-start | bytes 8388608 | tf_op jit(solution)/shard_map/all_to_all | solution.py:72
  402.8 8.8 copy-start.12
  450.1 51.9 %all-to-all-start.2 = ((f32[1,64,128,128]{3,2,0,1:T(8,128)}), f32[1,64,128,128]{3,2,0,1:T(8,128)}, u32[]{:S(2)}, u32[]{:S(2)}) async-start(f32[1,64,128,128]{3,2,0,1:T(8,128)} %subtract_bitcast_fusion.4), calls=%async_computation.2 | async-start | bytes 8388608 | tf_op jit(solution)/shard_map/all_to_all | solution.py:71
  455.1 309.8 %all-reduce.7.cloned.1.call-start = ((), (), s32[]{:S(2)}) async-start(), calls=%async_computation.8 | async-start | bytes 16777216 | tf_op jit(solution)/shard_map/psum | solution.py:90
  512.9 13.0 %copy-start.17 = (f32[16,512,128]{1,2,0:T(8,128)S(1)}, f32[16,512,128]{1,2,0:T(8,128)}, u32[]{:S(2)}) copy-start(f32[16,512,128]{1,2,0:T(8,128)} %reshape.464) | copy-start | bytes 12582916
  775.2 8.4 copy-start.22
  796.2 13.5 %copy-start.13 = (f32[64,128,128]{2,0,1:T(8,128)}, f32[64,128,128]{2,0,1:T(8,128)S(1)}, u32[]{:S(2)}) copy-start(f32[64,128,128]{2,0,1:T(8,128)S(1)} %subtract_bitcast_fusion.3) | copy-start | bytes 12582916
  802.7 7.1 copy-start.20
  818.0 52.4 %all-to-all-start.5 = ((f32[1,64,128,128]{3,2,0,1:T(8,128)}), f32[1,64,128,128]{3,2,0,1:T(8,128)}, u32[]{:S(2)}, u32[]{:S(2)}) async-start(f32[1,64,128,128]{3,2,0,1:T(8,128)} %add_bitcast_fusion.2), calls=%async_computation.5 | async-start | bytes 8388608 | tf_op jit(solution)/shard_map/all_to_all | solution.py:72
  823.2 8.8 copy-start.14
  870.4 51.9 %all-to-all-start.4 = ((f32[1,64,128,128]{3,2,0,1:T(8,128)}), f32[1,64,128,128]{3,2,0,1:T(8,128)}, u32[]{:S(2)}, u32[]{:S(2)}) async-start(f32[1,64,128,128]{3,2,0,1:T(8,128)} %subtract_bitcast_fusion.2), calls=%async_computation.4 | async-start | bytes 8388608 | tf_op jit(solution)/shard_map/all_to_all | solution.py:71
  933.2 13.0 %copy-start.18 = (f32[16,512,128]{1,2,0:T(8,128)S(1)}, f32[16,512,128]{1,2,0:T(8,128)}, u32[]{:S(2)}) copy-start(f32[16,512,128]{1,2,0:T(8,128)} %reshape.470) | copy-start | bytes 12582916
  988.1 24.6 %copy-start.23 = (f32[1,3]{1,0:T(1,128)}, f32[1,3]{1,0:T(1,128)S(1)}, u32[]{:S(2)}) copy-start(f32[1,3]{1,0:T(1,128)S(1)} %broadcast_divide_fusion) | copy-start | bytes 40
  990.8 21.9 %copy-start = (f32[128,128,64]{1,2,0:T(8,128)S(1)}, f32[128,128,64]{1,2,0:T(8,128)}, u32[]{:S(2)}) copy-start(f32[128,128,64]{1,2,0:T(8,128)} %convolution_add_fusion) | copy-start | bytes 12582916
  990.8 21.9 %copy-start.1 = (f32[128,128,64]{1,2,0:T(8,128)S(1)}, f32[128,128,64]{1,2,0:T(8,128)}, u32[]{:S(2)}) copy-start(f32[128,128,64]{1,2,0:T(8,128)} %convolution_subtract_fusion) | copy-start | bytes 12582916
  1052.2 27.2 %copy-start.6 = (f32[64,128,128]{2,0,1:T(8,128)}, f32[64,128,128]{2,0,1:T(8,128)S(1)}, u32[]{:S(2)}) copy-start(f32[64,128,128]{2,0,1:T(8,128)S(1)} %subtract_bitcast_fusion.1) | copy-start | bytes 12582916
  1072.3 7.1 copy-start.10
  1087.6 47.1 %all-to-all-start.7 = ((f32[1,64,128,128]{3,2,0,1:T(8,128)}), f32[1,64,128,128]{3,2,0,1:T(8,128)}, u32[]{:S(2)}, u32[]{:S(2)}) async-start(f32[1,64,128,128]{3,2,0,1:T(8,128)} %add_bitcast_fusion), calls=%async_computation.7 | async-start | bytes 8388608 | tf_op jit(solution)/shard_map/all_to_all | solution.py:72
  1092.7 8.8 copy-start.7
  1134.8 51.8 %all-to-all-start.6 = ((f32[1,64,128,128]{3,2,0,1:T(8,128)}), f32[1,64,128,128]{3,2,0,1:T(8,128)}, u32[]{:S(2)}, u32[]{:S(2)}) async-start(f32[1,64,128,128]{3,2,0,1:T(8,128)} %subtract_bitcast_fusion), calls=%async_computation.6 | async-start | bytes 8388608 | tf_op jit(solution)/shard_map/all_to_all | solution.py:71
  1197.5 13.0 %copy-start.15 = (f32[16,512,128]{1,2,0:T(8,128)S(1)}, f32[16,512,128]{1,2,0:T(8,128)}, u32[]{:S(2)}) copy-start(f32[16,512,128]{1,2,0:T(8,128)} %reshape.476) | copy-start | bytes 12582916
  (2 other events, 6.1 us)
Sparse Core Ops, SparseCore 0:
  168.4 175.9 all-reduce.8
  589.8 174.9 all-reduce.6
where the time goes:
time: 1250 us; the launch traced here: 1240 us
  waiting for transfers between devices  617 us (49%)
  matrix products  373 us (30%)
  local copies, waits for them, and re-layouts  87.9 us (7%)
  other arithmetic  59.8 us (5%)
  starting transfers between devices  40.9 us (3%)
  blocking collectives  38 us (3%)
  between operations  19.1 us (2%)
    psum x2, waiting for transfers between devices, template_sum(): lax.psum((jnp.sum(spectrum[0], axis=0), jnp.sum(spectrum[1], axis=0)), 'tm')  351 us
    dot_general x16, matrix products, mix_z(): return jnp.einsum('kz,vz...->vk...', table, data, precision=precise)  157 us
    dot_general x16, matrix products, mix_y(): return jnp.dot(data, table, precision=precise)  115 us
    all_to_all x3, waiting for transfers between devices, inverse(): lax.all_to_all(real_y, 'space', split_axis=1, concat_axis=2, tiled=True)  109 us
    dot_general x8, matrix products, mix_x(): return jnp.einsum('kx,vzx...->vzk...', table, data, precision=precise)  102 us
    all_to_all x3, waiting for transfers between devices, inverse(): lax.all_to_all(imag_y, 'space', split_axis=1, concat_axis=2, tiled=True)  85.7 us
    all_to_all x1, waiting for transfers between devices, forward(): lax.all_to_all(imag_y, 'space', split_axis=2, concat_axis=1, tiled=True)  36.6 us
    all_to_all x1, waiting for transfers between devices, forward(): lax.all_to_all(real_y, 'space', split_axis=2, concat_axis=1, tiled=True)  34.3 us
  transfers between devices with their start and end apart: 10, of which 10 were waited for; matrix products, arithmetic and copies ran while one was open for 9% of the time, Pallas kernels for 0%

commit v1 on v0

v1 whole, which is shorter than its diff:
```python
import math

import jax
import jax.numpy as jnp
from jax import lax
from jax.sharding import PartitionSpec as P

X = 512
Y = 128
Z = 64
ITERS = 2
HALF = X // 2

precise = lax.Precision.HIGHEST
sharpness = 256.0
floor_share = 0.05


def angles(rows, cols, length):
    products = rows[:, None] * cols[None, :] % length
    return products.astype(jnp.float32) * (2.0 * math.pi / length)


def x_tables():
    k = jnp.arange(HALF, dtype=jnp.int32)
    n = jnp.arange(X, dtype=jnp.int32)
    theta = angles(k, n, X)
    cos = jnp.cos(theta)
    sin = jnp.sin(theta)
    alt = jnp.where(n % 2 == 0, 1.0, -1.0).astype(jnp.float32)[None, :]
    first = (k == 0)[:, None]
    fwd = jnp.concatenate([cos, jnp.where(first, alt, -sin)], axis=0)
    norming = 1.0 / (X * Y * Z)
    inv_re = jnp.where(first, 1.0, 2.0 * cos) * norming
    inv_im = jnp.where(first, alt, -2.0 * sin) * norming
    inv = jnp.concatenate([inv_re, inv_im], axis=0).T
    return fwd, inv


def y_tables():
    k = jnp.arange(Y, dtype=jnp.int32)
    theta = angles(k, k, Y)
    return jnp.cos(theta), jnp.sin(theta)


def z_tables():
    k = jnp.arange(Z, dtype=jnp.int32)
    theta = angles(k, k, Z)
    c = jnp.cos(theta)
    s = jnp.sin(theta)
    fwd = jnp.stack([jnp.stack([c, s], axis=-1), jnp.stack([-s, c], axis=-1)], axis=1)
    inv = jnp.stack([jnp.stack([c, -s], axis=-1), jnp.stack([s, c], axis=-1)], axis=1)
    return fwd.reshape(2 * Z, 2 * Z), inv.reshape(2 * Z, 2 * Z)


def signed_freq(indices, length):
    wrapped = jnp.where(indices < length // 2, indices, indices - length)
    return jnp.where(indices == length // 2, 0, wrapped).astype(jnp.float32)


def centred(indices, length):
    return ((indices + length // 2) % length - length // 2).astype(jnp.float32)


def dot_y(data, table):
    return jnp.einsum("...y,yk->...k", data, table, precision=precise)


def mix_z(table, data):
    v, nz, two, nk, ny = data.shape
    flat = data.reshape(v, nz * two, nk * ny)
    out = jnp.einsum("pq,vqr->vpr", table, flat, precision=precise)
    return out.reshape(v, nz, two, nk, ny)


def forward(volume, tables):
    x_fwd, _, cos_y, sin_y, z_fwd, _ = tables
    v, nz = volume.shape[0], volume.shape[1]
    a = jnp.einsum("qn,vzny->vzqy", x_fwd, volume, precision=precise)
    a = a.reshape(v, nz, 2, HALF, Y)
    re, im = a[:, :, 0], a[:, :, 1]
    a = jnp.stack(
        [dot_y(re, cos_y) + dot_y(im, sin_y), dot_y(im, cos_y) - dot_y(re, sin_y)], axis=2
    )
    a = lax.all_to_all(a, "space", split_axis=3, concat_axis=1, tiled=True)
    return mix_z(z_fwd, a)


def mirror(col):
    return jnp.roll(jnp.flip(col, axis=(1, 3)), 1, axis=(1, 3))


def unpack(spectrum, first):
    col = spectrum[:, :, :, 0, :]
    mir = mirror(col)
    c_re, c_im = col[:, :, 0], col[:, :, 1]
    m_re, m_im = mir[:, :, 0], mir[:, :, 1]
    low = jnp.stack([(c_re + m_re) * 0.5, (c_im - m_im) * 0.5], axis=2)
    nyq = jnp.stack([(c_im + m_im) * 0.5, (m_re - c_re) * 0.5], axis=2)
    spectrum = spectrum.at[:, :, :, 0, :].set(jnp.where(first, low, col))
    return spectrum, jnp.where(first, nyq, 0.0)


def pack(spectrum, nyq):
    col = spectrum[:, :, :, 0, :]
    packed = jnp.stack([col[:, :, 0] - nyq[:, :, 1], col[:, :, 1] + nyq[:, :, 0]], axis=2)
    return spectrum.at[:, :, :, 0, :].set(packed)


def inverse(spectrum, nyq, tables):
    _, x_inv, cos_y, sin_y, _, z_inv = tables
    a = mix_z(z_inv, pack(spectrum, nyq))
    re, im = a[:, :, 0], a[:, :, 1]
    a = jnp.stack(
        [dot_y(re, cos_y) - dot_y(im, sin_y), dot_y(re, sin_y) + dot_y(im, cos_y)], axis=2
    )
    a = lax.all_to_all(a, "space", split_axis=1, concat_axis=3, tiled=True)
    v, nz = a.shape[0], a.shape[1]
    a = a.reshape(v, nz, 2 * HALF, Y)
    return jnp.einsum("nq,vzqy->vzny", x_inv, a, precision=precise)


def whiten(spec, tmpl):
    s_re, s_im = spec[:, :, 0], spec[:, :, 1]
    t_re, t_im = tmpl[:, :, 0], tmpl[:, :, 1]
    prod_re = s_re * t_re + s_im * t_im
    prod_im = s_im * t_re - s_re * t_im
    divisor = jnp.maximum(
        jnp.sqrt(prod_re * prod_re + prod_im * prod_im), floor_share * (X * Y * Z)
    )
    return jnp.stack([prod_re / divisor, prod_im / divisor], axis=2)


def weight_moments(weights, coords):
    coord_z, coord_x, coord_y = coords
    weight_sum = jnp.sum(weights, axis=(1, 2, 3))
    moment_z = jnp.sum(jnp.sum(weights, axis=(2, 3)) * coord_z[None, :], axis=1)
    moment_x = jnp.sum(jnp.sum(weights, axis=(1, 3)) * coord_x[None, :], axis=1)
    moment_y = jnp.sum(jnp.sum(weights, axis=(1, 2)) * coord_y[None, :], axis=1)
    return (weight_sum, jnp.stack([moment_z, moment_x, moment_y], axis=1))


def centroid(scores, coords):
    local_top = jnp.max(scores, axis=(1, 2, 3))
    top_score = lax.pmax(local_top, "space")
    weights = jnp.exp(scores - top_score[:, None, None, None])
    weight_sum, moments = weight_moments(weights, coords)
    weight_sum, moments = lax.psum((weight_sum, moments), "space")
    return moments / weight_sum[:, None]


def unit(phase):
    return jnp.cos(phase), jnp.sin(phase)


def cmul(a, b):
    return (a[0] * b[0] - a[1] * b[1], a[0] * b[1] + a[1] * b[0])


def apply_ramp(spec, nyq, shifts, freq_z, freq_x, freq_y):
    ez = unit(2.0 * math.pi * freq_z[None, :] * (shifts[:, 0] / Z)[:, None])
    ex = unit(2.0 * math.pi * freq_x[None, :] * (shifts[:, 1] / X)[:, None])
    ey = unit(2.0 * math.pi * freq_y[None, :] * (shifts[:, 2] / Y)[:, None])
    exy = cmul((ex[0][:, :, None], ex[1][:, :, None]), (ey[0][:, None, :], ey[1][:, None, :]))
    ezy = cmul((ez[0][:, :, None], ez[1][:, :, None]), (ey[0][:, None, :], ey[1][:, None, :]))
    e = cmul((ez[0][:, :, None, None], ez[1][:, :, None, None]), (exy[0][:, None], exy[1][:, None]))
    main = cmul((spec[:, :, 0], spec[:, :, 1]), e)
    edge = cmul((nyq[:, :, 0], nyq[:, :, 1]), ezy)
    return jnp.stack(main, axis=2), jnp.stack(edge, axis=2)


def body(volumes):
    position = lax.axis_index("space")
    first = position == 0
    slab_depth = volumes.shape[1]
    pencil = HALF // lax.axis_size("space")
    frames = volumes.shape[0] * lax.axis_size("tm")
    tables = x_tables() + y_tables() + z_tables()
    z_index = position * slab_depth + jnp.arange(slab_depth, dtype=jnp.int32)
    x_index = position * pencil + jnp.arange(pencil, dtype=jnp.int32)
    coords = (
        centred(z_index, Z),
        centred(jnp.arange(X, dtype=jnp.int32), X),
        centred(jnp.arange(Y, dtype=jnp.int32), Y),
    )
    freq_z = signed_freq(jnp.arange(Z, dtype=jnp.int32), Z)
    freq_x = x_index.astype(jnp.float32)
    freq_y = signed_freq(jnp.arange(Y, dtype=jnp.int32), Y)
    spec, spec_nyq = unpack(forward(volumes, tables), first)
    shifted, shifted_nyq = spec, spec_nyq
    for iteration in range(ITERS):
        summed, summed_nyq = lax.psum((jnp.sum(shifted, axis=0), jnp.sum(shifted_nyq, axis=0)), "tm")
        tmpl = summed[None] / frames
        tmpl_nyq = summed_nyq[None] / frames
        white = whiten(spec, tmpl)
        white_nyq = whiten(spec_nyq, tmpl_nyq)
        correlation = inverse(white, white_nyq, tables)
        shifts = centroid(sharpness * correlation, coords)
        shifted, shifted_nyq = apply_ramp(spec, spec_nyq, shifts, freq_z, freq_x, freq_y)
    corrected = inverse(shifted, shifted_nyq, tables)
    return (corrected, shifts)


def solution(mesh):
    in_specs = (P("tm", "space", None, None),)
    out_specs = (P("tm", "space", None, None), P("tm", None))
    return jax.shard_map(body, mesh=mesh, in_specs=in_specs, out_specs=out_specs, check_vma=False)
```

time: 1250 us -> 780 us (0.62)
  waiting for transfers between devices: 617 us -> 277 us
  matrix products: 373 us -> 121 us
  blocking collectives: 38 us -> 135 us
  other arithmetic: 59.8 us -> 116 us
  starting transfers between devices: 40.9 us -> 10.1 us
    dot_general x40 -> x24, matrix products: 373 us -> 121 us  [the longest x4 46.5 us: mix_z(): out = jnp.einsum('pq,vqr->vpr', table, flat, precision=precise)]
    all_to_all x8 -> x2, waiting for transfers between devices: 265 us -> 88.4 us  [the longest x1 47.4 us: inverse(): a = lax.all_to_all(a, 'space', split_axis=1, concat_axis=3, tiled=True)]
    psum x2, waiting for transfers between devices: 351 us -> 189 us  [body(): lax.psum((jnp.sum(shifted, axis=0), jnp.sum(shifted_nyq, axis=0)), 'tm')]
    all_to_all x0 -> x2, blocking collectives: none -> 97 us  [inverse(): a = lax.all_to_all(a, 'space', split_axis=1, concat_axis=3, tiled=True)]
    transpose x0 -> x4, local copies, waits for them, and re-layouts: none -> 39.2 us  [mix_z(): out = jnp.einsum('pq,vqr->vpr', table, flat, precision=precise)]
    div x0 -> x8, other arithmetic: none -> 37.7 us  [the longest x4 28.6 us: whiten(): return jnp.stack([prod_re / divisor, prod_im / divisor], axis=2)]
    all_to_all x8 -> x2, starting transfers between devices: 40.6 us -> 10.1 us  [the longest x1 5.19 us: forward(): a = lax.all_to_all(a, 'space', split_axis=3, concat_axis=1, tiled=True)]
    all_to_all x8 -> x4, local copies, waits for them, and re-layouts: 37.2 us -> 8.26 us  [the longest x1 4.62 us: forward(): a = lax.all_to_all(a, 'space', split_axis=3, concat_axis=1, tiled=True)]
  transfers between devices with their start and end apart: 10 -> 4, of which waited for: 10 -> 4; matrix products, arithmetic and copies ran while one was open for 9% -> 2% of each run, Pallas kernels for 0% -> 0%
where the time goes in v1:
time: 780 us; the launch traced here: 772 us
  waiting for transfers between devices  277 us (36%)
  blocking collectives  135 us (17%)
  matrix products  121 us (16%)
  other arithmetic  116 us (15%)
  local copies, waits for them, and re-layouts  94.4 us (12%)
  between operations  18.9 us (2%)
  starting transfers between devices  10.1 us (1%)
    psum x2, waiting for transfers between devices, body(): lax.psum((jnp.sum(shifted, axis=0), jnp.sum(shifted_nyq, axis=0)), 'tm')  189 us
    all_to_all x2, blocking collectives, inverse(): a = lax.all_to_all(a, 'space', split_axis=1, concat_axis=3, tiled=True)  97 us
    all_to_all x1, waiting for transfers between devices, inverse(): a = lax.all_to_all(a, 'space', split_axis=1, concat_axis=3, tiled=True)  47.4 us
    dot_general x4, matrix products, mix_z(): out = jnp.einsum('pq,vqr->vpr', table, flat, precision=precise)  46.5 us
    all_to_all x1, waiting for transfers between devices, forward(): a = lax.all_to_all(a, 'space', split_axis=3, concat_axis=1, tiled=True)  41 us
    transpose x4, local copies, waits for them, and re-layouts, mix_z(): out = jnp.einsum('pq,vqr->vpr', table, flat, precision=precise)  39.2 us
    dot_general x16, matrix products, dot_y(): return jnp.einsum('...y,yk->...k', data, table, precision=precise)  38.7 us
    div x4, other arithmetic, whiten(): return jnp.stack([prod_re / divisor, prod_im / divisor], axis=2)  28.6 us
  transfers between devices with their start and end apart: 4, of which 4 were waited for; matrix products, arithmetic and copies ran while one was open for 2% of the time, Pallas kernels for 0%

profile of v1, /device:TPU:0, one launch (start us, length us, event | category | flops | bytes accessed | tf_op | source)
XLA Modules:
  0.0 772.2 jit_solution(13888175762530893939)
XLA Ops:
  11.3 9.0 %fusion.8 = f32[512,16,128]{2,0,1:T(8,128)S(1)} fusion(f32[1,16,512,128]{3,2,1,0:T(8,128)} %param.9, f32[256,512]{1,0:T(8,128)S(1)} %get-tuple-element.114, f32[256,512]{1,0:T(8,128)S(1)} %fusion.46), kind=kOutput, calls=%fused_computation.26 | convolution fusion | flops 6442713088 | bytes 9437184 | tf_op jit(solution)/shard_map/qn,vzny->vzqy/dot_general | solution.py:79
  46.5 41.0 %all-to-all-done = f32[1,16,2,256,128]{4,1,2,0,3:T(8,128)} async-done(((f32[1,16,2,256,128]{4,1,2,0,3:T(8,128)}), f32[1,16,2,256,128]{4,1,2,0,3:T(8,128)}, u32[]{:S(2)}, u32[]{:S(2)}) %all-to-all-start) | async-done | bytes 4194336 | tf_op jit(solution)/shard_map/all_to_all | solution.py:85
  92.1 11.5 %convolution_bitcast_fusion.3 = f32[1,128,8192]{1,2,0:T(8,128)} fusion(f32[128,128]{1,0:T(8,128)S(1)} %reshape.1850, f32[16,8,64,128]{3,2,1,0:T(8,128)S(1)} %bitcast.289), kind=kOutput, calls=%fused_computation.3 | convolution fusion | flops 1610612736 | bytes 8454144 | tf_op jit(solution)/shard_map/pq,vqr->vpr/dot_general | solution.py:72
  103.5 9.8 %copy.211 = f32[1,128,8192]{2,0,1:T(1,128)} copy(f32[1,128,8192]{1,2,0:T(8,128)} %convolution_bitcast_fusion.3) | data formatting | bytes 8388608 | tf_op jit(solution)/shard_map/pq,vqr->vpr/transpose | solution.py:72
  114.4 7.4 copy.213
  130.5 91.6 %all-reduce.9.cloned.1.call-done = (f32[64,2,64,128]{3,1,0,2:T(2,128)}, f32[64,2,128]{2,1,0:T(2,128)}) async-done(((f32[64,2,64,128]{3,1,0,2:T(2,128)}, f32[64,2,128]{2,1,0:T(2,128)}), (f32[64,2,64,128]{3,1,0,2:T(2,128)}, f32[64,2,128]{2,1,0:T(2,128)})) %all-reduce.9.cloned.1.call-update) | async-done | bytes 4259856 | tf_op jit(solution)/shard_map/psum | solution.py:192
  226.6 7.6 slice_multiply_fusion
  237.6 7.2 fusion.198
  253.1 12.0 %convolution_bitcast_fusion.2 = f32[1,128,8192]{1,2,0:T(8,128)} fusion(f32[128,128]{1,0:T(8,128)S(1)} %reshape.1854, f32[16,8,64,128]{3,2,1,0:T(8,128)} %bitcast.288), kind=kOutput, calls=%fused_computation.2 | convolution fusion | flops 1610612736 | bytes 8454144 | tf_op jit(solution)/shard_map/pq,vqr->vpr/dot_general | solution.py:72
  265.1 10.0 %copy.229 = f32[1,128,8192]{2,0,1:T(1,128)} copy(f32[1,128,8192]{1,2,0:T(8,128)} %convolution_bitcast_fusion.2) | data formatting | bytes 8388608 | tf_op jit(solution)/shard_map/pq,vqr->vpr/transpose | solution.py:72
  293.1 47.4 %all-to-all-done.1 = f32[1,64,2,64,128]{4,3,2,0,1:T(8,128)} async-done(((f32[1,64,2,64,128]{4,3,2,0,1:T(8,128)}), f32[1,64,2,64,128]{4,3,2,0,1:T(8,128)}, u32[]{:S(2)}, u32[]{:S(2)}) %all-to-all-start.1) | async-done | bytes 4194336 | tf_op jit(solution)/shard_map/all_to_all | solution.py:117
  343.0 9.1 %multiply_reduce_fusion.1 = (f32[]{:T(128)}, f32[16,128,512]{2,1,0:T(8,128)}) fusion(f32[16,512,128]{2,1,0:T(8,128)S(1)} %bitcast.294, f32[256,512]{1,0:T(8,128)S(1)} %get-tuple-element.113, f32[256,512]{1,0:T(8,128)S(1)} %get-tuple-element.125), kind=kOutput, calls=%fused_computation.33 | convolution fusion | flops 6444810240 | bytes 9437188 | tf_op jit(solution)/shard_map/nq,vzqy->vzny/dot_general | solution.py:120
  352.1 9.5 %pmax.14 = f32[]{:T(128)} all-reduce(f32[]{:T(128)} %get-tuple-element.126), channel_id=1, replica_groups=mesh['tm'=8,'space'=4] {'space'}, use_global_device_ids=true, to_apply=%region_3.4 | all-reduce | flops 1 | bytes 8 | tf_op jit(solution)/shard_map/pmax | solution.py:145
  361.5 5.6 fusion.27
  370.9 9.7 %all-reduce.3 = (f32[1,3]{1,0:T(1,128)S(1)}, f32[]{:T(128)}) all-reduce(f32[1,3]{1,0:T(1,128)S(1)} %pad_maximum_fusion.15, f32[]{:T(128)} %get-tuple-element.66), channel_id=1, replica_groups=mesh['tm'=8,'space'=4] {'space'}, use_global_device_ids=true, to_apply=%region_10.11 | all-reduce | flops 4 | bytes 32 | tf_op jit(solution)/shard_map/psum | solution.py:148
  385.3 9.9 %multiply_subtract_fusion.3 = (f32[1,64,1,64,128]{4,2,1,3,0:T(1,128)S(1)}, f32[1,64,1,64,128]{4,2,1,3,0:T(1,128)S(1)}) fusion(f32[64,128]{1,0:T(8,128)S(1)} %get-tuple-element.118, f32[64]{0:T(128)S(1)} %multiply_sine_fusion.3, f32[64,128]{1,0:T(8,128)S(1)} %get-tuple-element.117, f32[64]{0:T(128)S(1)} %multiply_cosine_fusion.3, ...), kind=kLoop, calls=%fused_computation.60 | loop fusion | flops 6291456 | bytes 8454656 | tf_op jit(solution)/shard_map/sub | solution.py:157
  395.1 6.3 maximum_bitcast_fusion
  401.4 97.1 %all-reduce.7.cloned.1.call-done = (f32[64,2,64,128]{3,1,0,2:T(2,128)}, f32[64,2,128]{2,1,0:T(2,128)}) async-done(((f32[64,2,64,128]{3,1,0,2:T(2,128)}, f32[64,2,128]{2,1,0:T(2,128)}), (f32[64,2,64,128]{3,1,0,2:T(2,128)}, f32[64,2,128]{2,1,0:T(2,128)})) %all-reduce.7.cloned.1.call-update) | async-done | bytes 4259856 | tf_op jit(solution)/shard_map/psum | solution.py:192
  503.1 12.6 %fusion.197 = (f32[1,64,1,64,128]{4,2,1,3,0:T(1,128)S(1)}, f32[1,64,1,64,128]{4,2,1,3,0:T(1,128)S(1)}, f32[1,64,1,64,128]{4,2,1,3,0:T(1,128)S(1)}) fusion(f32[1,64,2,64,128]{4,2,1,3,0:T(2,128)S(1)} %multiply_bitcast_fusion, f32[1,64,2,64,128]{4,2,1,3,0:T(2,128)S(1)} %copy-done.1), kind=kLoop, calls=%fused_computation.338 | loop fusion | flops 5767168 | bytes 14680064 | tf_op jit(solution)/shard_map/div | solution.py:131
  515.7 7.5 fusion.196
  530.4 11.5 %convolution_bitcast_fusion.1 = f32[1,128,8192]{1,2,0:T(8,128)} fusion(f32[128,128]{1,0:T(8,128)S(1)} %reshape.1854, f32[16,8,64,128]{3,2,1,0:T(8,128)S(1)} %bitcast.291), kind=kOutput, calls=%fused_computation.1 | convolution fusion | flops 1610612736 | bytes 8454144 | tf_op jit(solution)/shard_map/pq,vqr->vpr/dot_general | solution.py:72
  541.9 9.8 %copy.240 = f32[1,128,8192]{2,0,1:T(1,128)} copy(f32[1,128,8192]{1,2,0:T(8,128)} %convolution_bitcast_fusion.1) | data formatting | bytes 8388608 | tf_op jit(solution)/shard_map/pq,vqr->vpr/transpose | solution.py:72
  563.0 51.3 %all_to_all.60 = f32[1,64,2,64,128]{4,3,2,0,1:T(8,128)S(1)} all-to-all(f32[1,64,2,64,128]{4,3,2,0,1:T(8,128)S(1)} %copy.243), channel_id=1, replica_groups=mesh['tm'=8,'space'=4] {'space'}, dimensions={1} | all-to-all | bytes 8388608 | tf_op jit(solution)/shard_map/all_to_all | solution.py:117
  614.9 8.9 %multiply_reduce_fusion = (f32[]{:T(128)}, f32[16,128,512]{2,1,0:T(8,128)}) fusion(f32[16,512,128]{2,1,0:T(8,128)S(1)} %bitcast.295, f32[256,512]{1,0:T(8,128)S(1)} %get-tuple-element.113, f32[256,512]{1,0:T(8,128)S(1)} %get-tuple-element.125), kind=kOutput, calls=%fused_computation.32 | convolution fusion | flops 6444810240 | bytes 9437188 | tf_op jit(solution)/shard_map/nq,vzqy->vzny/dot_general | solution.py:120
  623.8 9.0 %pmax.15 = f32[]{:T(128)} all-reduce(f32[]{:T(128)} %get-tuple-element.128), channel_id=1, replica_groups=mesh['tm'=8,'space'=4] {'space'}, use_global_device_ids=true, to_apply=%region_16.17 | all-reduce | flops 1 | bytes 8 | tf_op jit(solution)/shard_map/pmax | solution.py:145
  632.8 5.6 fusion.31
  642.1 9.9 %all-reduce.2 = (f32[1,3]{1,0:T(1,128)S(1)}, f32[]{:T(128)}) all-reduce(f32[1,3]{1,0:T(1,128)S(1)} %pad_maximum_fusion.16, f32[]{:T(128)} %get-tuple-element.62), channel_id=1, replica_groups=mesh['tm'=8,'space'=4] {'space'}, use_global_device_ids=true, to_apply=%region_23.24 | all-reduce | flops 4 | bytes 32 | tf_op jit(solution)/shard_map/psum | solution.py:148
  655.6 9.9 %multiply_subtract_fusion = (f32[1,64,1,64,128]{4,2,1,3,0:T(1,128)S(1)}, f32[1,64,1,64,128]{4,2,1,3,0:T(1,128)S(1)}) fusion(f32[64,128]{1,0:T(8,128)S(1)} %get-tuple-element.116, f32[64]{0:T(128)S(1)} %multiply_sine_fusion.1, f32[64,128]{1,0:T(8,128)S(1)} %get-tuple-element.115, f32[64]{0:T(128)S(1)} %multiply_cosine_fusion.1, ...), kind=kLoop, calls=%fused_computation.51 | loop fusion | flops 6291456 | bytes 8454656 | tf_op jit(solution)/shard_map/sub | solution.py:157
  672.6 11.6 %convolution_bitcast_fusion = f32[1,128,8192]{1,2,0:T(8,128)} fusion(f32[128,128]{1,0:T(8,128)S(1)} %reshape.1854, f32[16,8,64,128]{3,2,1,0:T(8,128)S(1)} %bitcast.290), kind=kOutput, calls=%fused_computation | convolution fusion | flops 1610612736 | bytes 8454144 | tf_op jit(solution)/shard_map/pq,vqr->vpr/dot_general | solution.py:72
  684.2 9.6 %copy.251 = f32[1,128,8192]{2,0,1:T(1,128)} copy(f32[1,128,8192]{1,2,0:T(8,128)} %convolution_bitcast_fusion) | data formatting | bytes 8388608 | tf_op jit(solution)/shard_map/pq,vqr->vpr/transpose | solution.py:72
  705.2 45.8 %all_to_all.61 = f32[1,64,2,64,128]{4,3,2,0,1:T(8,128)S(1)} all-to-all(f32[1,64,2,64,128]{4,3,2,0,1:T(8,128)S(1)} %copy.254), channel_id=1, replica_groups=mesh['tm'=8,'space'=4] {'space'}, dimensions={1} | all-to-all | bytes 8388608 | tf_op jit(solution)/shard_map/all_to_all | solution.py:117
  751.5 8.3 %convolution_bitcast_fusion.4 = f32[1,16,512,128]{2,3,1,0:T(8,128)} fusion(f32[16,512,128]{2,1,0:T(8,128)S(1)} %bitcast.296, f32[256,512]{1,0:T(8,128)S(1)} %get-tuple-element.113, f32[256,512]{1,0:T(8,128)S(1)} %get-tuple-element.125), kind=kOutput, calls=%fused_computation.34 | convolution fusion | flops 6442713088 | bytes 9437184 | tf_op jit(solution)/shard_map/nq,vzqy->vzny/dot_general | solution.py:120
  (132 shorter events, 140.5 us)
Async XLA Ops:
  33.6 53.8 %all-to-all-start = ((f32[1,16,2,256,128]{4,1,2,0,3:T(8,128)}), f32[1,16,2,256,128]{4,1,2,0,3:T(8,128)}, u32[]{:S(2)}, u32[]{:S(2)}) async-start(f32[1,16,2,256,128]{4,1,2,0,3:T(8,128)} %copy.208), calls=%async_computation | async-start | bytes 8388608 | tf_op jit(solution)/shard_map/all_to_all | solution.py:85
  38.8 183.2 %all-reduce.9.cloned.1.call-start = ((), (), s32[]{:S(2)}) async-start(), calls=%async_computation.5 | async-start | bytes 8519680 | tf_op jit(solution)/shard_map/psum | solution.py:192
  222.1 4.5 copy-start
  247.4 2.3 copy-start.5
  275.1 3.9 copy-start.2
  288.2 52.3 %all-to-all-start.1 = ((f32[1,64,2,64,128]{4,3,2,0,1:T(8,128)}), f32[1,64,2,64,128]{4,3,2,0,1:T(8,128)}, u32[]{:S(2)}, u32[]{:S(2)}) async-start(f32[1,64,2,64,128]{4,3,2,0,1:T(8,128)} %copy.232), calls=%async_computation.1 | async-start | bytes 8388608 | tf_op jit(solution)/shard_map/all_to_all | solution.py:117
  293.0 205.5 %all-reduce.7.cloned.1.call-start = ((), (), s32[]{:S(2)}) async-start(), calls=%async_computation.4 | async-start | bytes 8519680 | tf_op jit(solution)/shard_map/psum | solution.py:192
  498.5 4.5 copy-start.1
  523.3 4.2 copy-start.6
  551.7 3.9 copy-start.3
  652.6 12.8 %copy-start.7 = (f32[1,3]{1,0:T(1,128)}, f32[1,3]{1,0:T(1,128)S(1)}, u32[]{:S(2)}) copy-start(f32[1,3]{1,0:T(1,128)S(1)} %broadcast_divide_fusion) | copy-start | bytes 40
  693.8 3.9 copy-start.4
Sparse Core Ops, SparseCore 0:
  123.8 98.2 all-reduce.8
  401.5 96.9 all-reduce.6

commit v2 on v1

--- a/solution.py
+++ b/solution.py
@@ -62,14 +62,14 @@
     return ((indices + length // 2) % length - length // 2).astype(jnp.float32)
 
 
-def dot_y(data, table):
-    return jnp.einsum("...y,yk->...k", data, table, precision=precise)
-
-
-def mix_z(table, data):
+def dot_y(data, table, precision=precise):
+    return jnp.einsum("...y,yk->...k", data, table, precision=precision)
+
+
+def mix_z(table, data, precision=precise):
     v, nz, two, nk, ny = data.shape
     flat = data.reshape(v, nz * two, nk * ny)
-    out = jnp.einsum("pq,vqr->vpr", table, flat, precision=precise)
+    out = jnp.einsum("pq,vqr->vpr", table, flat, precision=precision)
     return out.reshape(v, nz, two, nk, ny)
 
 
@@ -107,17 +107,21 @@
     return spectrum.at[:, :, :, 0, :].set(packed)
 
 
-def inverse(spectrum, nyq, tables):
+def inverse(spectrum, nyq, tables, precision=precise):
     _, x_inv, cos_y, sin_y, _, z_inv = tables
-    a = mix_z(z_inv, pack(spectrum, nyq))
+    a = mix_z(z_inv, pack(spectrum, nyq), precision)
     re, im = a[:, :, 0], a[:, :, 1]
     a = jnp.stack(
-        [dot_y(re, cos_y) - dot_y(im, sin_y), dot_y(re, sin_y) + dot_y(im, cos_y)], axis=2
+        [
+            dot_y(re, cos_y, precision) - dot_y(im, sin_y, precision),
+            dot_y(re, sin_y, precision) + dot_y(im, cos_y, precision),
+        ],
+        axis=2,
     )
     a = lax.all_to_all(a, "space", split_axis=1, concat_axis=3, tiled=True)
     v, nz = a.shape[0], a.shape[1]
     a = a.reshape(v, nz, 2 * HALF, Y)
-    return jnp.einsum("nq,vzqy->vzny", x_inv, a, precision=precise)
+    return jnp.einsum("nq,vzqy->vzny", x_inv, a, precision=precision)
 
 
 def whiten(spec, tmpl):
@@ -142,11 +146,13 @@
 
 def centroid(scores, coords):
     local_top = jnp.max(scores, axis=(1, 2, 3))
-    top_score = lax.pmax(local_top, "space")
-    weights = jnp.exp(scores - top_score[:, None, None, None])
+    weights = jnp.exp(scores - local_top[:, None, None, None])
     weight_sum, moments = weight_moments(weights, coords)
-    weight_sum, moments = lax.psum((weight_sum, moments), "space")
-    return moments / weight_sum[:, None]
+    local = jnp.concatenate([local_top[:, None], weight_sum[:, None], moments], axis=1)
+    gathered = lax.all_gather(local, "space")
+    scale = jnp.exp(gathered[:, :, 0] - jnp.max(gathered[:, :, 0], axis=0)[None, :])
+    totals = jnp.sum(gathered[:, :, 1:] * scale[:, :, None], axis=0)
+    return totals[:, 1:] / totals[:, 0:1]
 
 
 def unit(phase):
@@ -197,7 +203,7 @@
         correlation = inverse(white, white_nyq, tables)
         shifts = centroid(sharpness * correlation, coords)
         shifted, shifted_nyq = apply_ramp(spec, spec_nyq, shifts, freq_z, freq_x, freq_y)
-    corrected = inverse(shifted, shifted_nyq, tables)
+    corrected = inverse(shifted, shifted_nyq, tables, lax.Precision.HIGH)
     return (corrected, shifts)
 
 

time: 780 us -> 746 us (0.956)
  blocking collectives: 135 us -> 114 us
  matrix products: 121 us -> 108 us
    psum x2 -> x0, blocking collectives: 19.6 us -> none  [centroid(): weight_sum, moments = lax.psum((weight_sum, moments), 'space')]
    pmax x2 -> x0, blocking collectives: 18.5 us -> none  [centroid(): top_score = lax.pmax(local_top, 'space')]
    all_gather x0 -> x2, blocking collectives: none -> 15.4 us  [centroid(): gathered = lax.all_gather(local, 'space')]
    dot_general x23, matrix products: 112 us -> 98.8 us  [the longest x4 43.6 us: mix_z(): out = jnp.einsum('pq,vqr->vpr', table, flat, precision=precision)]
    reduce_sum x2, other arithmetic: 11.2 us -> 0.19 us  [centroid(): totals = jnp.sum(gathered[:, :, 1:] * scale[:, :, None], axis=0)]
where the time goes in v2:
time: 746 us; the launch traced here: 739 us
  waiting for transfers between devices  277 us (37%)
  blocking collectives  114 us (15%)
  other arithmetic  110 us (15%)
  matrix products  108 us (14%)
  local copies, waits for them, and re-layouts  101 us (14%)
  between operations  19 us (3%)
  starting transfers between devices  10.5 us (1%)
    psum x2, waiting for transfers between devices, body(): lax.psum((jnp.sum(shifted, axis=0), jnp.sum(shifted_nyq, axis=0)), 'tm')  189 us
    all_to_all x2, blocking collectives, inverse(): a = lax.all_to_all(a, 'space', split_axis=1, concat_axis=3, tiled=True)  98.5 us
    all_to_all x1, waiting for transfers between devices, inverse(): a = lax.all_to_all(a, 'space', split_axis=1, concat_axis=3, tiled=True)  47 us
    dot_general x4, matrix products, mix_z(): out = jnp.einsum('pq,vqr->vpr', table, flat, precision=precision)  43.6 us
    all_to_all x1, waiting for transfers between devices, forward(): a = lax.all_to_all(a, 'space', split_axis=3, concat_axis=1, tiled=True)  41.2 us
    transpose x4, local copies, waits for them, and re-layouts, mix_z(): out = jnp.einsum('pq,vqr->vpr', table, flat, precision=precision)  39.3 us
    dot_general x16, matrix products, dot_y(): return jnp.einsum('...y,yk->...k', data, table, precision=precision)  35.3 us
    div x4, other arithmetic, whiten(): return jnp.stack([prod_re / divisor, prod_im / divisor], axis=2)  28.5 us
  transfers between devices with their start and end apart: 4, of which 4 were waited for; matrix products, arithmetic and copies ran while one was open for 2% of the time, Pallas kernels for 0%

profile of v2, /device:TPU:0, one launch (start us, length us, event | category | flops | bytes accessed | tf_op | source)
XLA Modules:
  0.0 738.6 jit_solution(3837708186419032451)
XLA Ops:
  11.3 9.0 %fusion.8 = f32[512,16,128]{2,0,1:T(8,128)S(1)} fusion(f32[1,16,512,128]{3,2,1,0:T(8,128)} %param.9, f32[256,512]{1,0:T(8,128)S(1)} %get-tuple-element.110, f32[256,512]{1,0:T(8,128)S(1)} %fusion.46), kind=kOutput, calls=%fused_computation.26 | convolution fusion | flops 6442713088 | bytes 9437184 | tf_op jit(solution)/shard_map/qn,vzny->vzqy/dot_general | solution.py:79
  33.6 5.2 all-to-all-start
  46.2 41.2 %all-to-all-done = f32[1,16,2,256,128]{4,1,2,0,3:T(8,128)} async-done(((f32[1,16,2,256,128]{4,1,2,0,3:T(8,128)}), f32[1,16,2,256,128]{4,1,2,0,3:T(8,128)}, u32[]{:S(2)}, u32[]{:S(2)}) %all-to-all-start) | async-done | bytes 4194336 | tf_op jit(solution)/shard_map/all_to_all | solution.py:85
  87.4 4.6 copy.209
  92.0 11.5 %convolution_bitcast_fusion.3 = f32[1,128,8192]{1,2,0:T(8,128)} fusion(f32[128,128]{1,0:T(8,128)S(1)} %reshape.1878, f32[16,8,64,128]{3,2,1,0:T(8,128)S(1)} %bitcast.301), kind=kOutput, calls=%fused_computation.3 | convolution fusion | flops 1610612736 | bytes 8454144 | tf_op jit(solution)/shard_map/pq,vqr->vpr/dot_general | solution.py:72
  103.5 10.0 %copy.211 = f32[1,128,8192]{2,0,1:T(1,128)} copy(f32[1,128,8192]{1,2,0:T(8,128)} %convolution_bitcast_fusion.3) | data formatting | bytes 8388608 | tf_op jit(solution)/shard_map/pq,vqr->vpr/transpose | solution.py:72
  114.6 7.4 %copy.213 = f32[1,64,2,64,128]{4,2,1,3,0:T(2,128)} copy(f32[1,64,2,64,128]{4,3,0,2,1:T(8,128)} %bitcast.304) | data formatting | bytes 8388608 | tf_op jit(solution)/shard_map/reshape | solution.py:73
  130.7 91.6 %all-reduce.7.cloned.1.call-done = (f32[64,2,64,128]{3,1,0,2:T(2,128)}, f32[64,2,128]{2,1,0:T(2,128)}) async-done(((f32[64,2,64,128]{3,1,0,2:T(2,128)}, f32[64,2,128]{2,1,0:T(2,128)}), (f32[64,2,64,128]{3,1,0,2:T(2,128)}, f32[64,2,128]{2,1,0:T(2,128)})) %all-reduce.7.cloned.1.call-update) | async-done | bytes 4259856 | tf_op jit(solution)/shard_map/psum | solution.py:198
  226.8 7.6 %slice_multiply_fusion = (f32[1,64,1,64,128]{4,2,1,3,0:T(1,128)S(1)}, f32[1,64,1,64,128]{4,2,1,3,0:T(1,128)S(1)}, f32[1,64,1,64,128]{4,2,1,3,0:T(1,128)S(1)}, f32[1,64,1,64,128]{4,2,1,3,0:T(1,128)S(1)}) fusion(f32[1,64,2,64,128]{4,2,1,3,0:T(2,128)S(1)} %multiply_bitcast_fusion.1, f32[1,64,2,64,128]{4,2,1,3,0:T(2,128)S(1)} %copy-done), kind=kLoop, calls=%fused_computation.93 | loop fusion | flops 2097152 | bytes 16777216 | tf_op jit(solution)/shard_map/mul | solution.py:130
  237.8 7.2 fusion.200
  253.3 12.2 %convolution_bitcast_fusion.2 = f32[1,128,8192]{1,2,0:T(8,128)} fusion(f32[128,128]{1,0:T(8,128)S(1)} %reshape.1882, f32[16,8,64,128]{3,2,1,0:T(8,128)} %bitcast.300), kind=kOutput, calls=%fused_computation.2 | convolution fusion | flops 1610612736 | bytes 8454144 | tf_op jit(solution)/shard_map/pq,vqr->vpr/dot_general | solution.py:72
  265.4 9.6 %copy.229 = f32[1,128,8192]{2,0,1:T(1,128)} copy(f32[1,128,8192]{1,2,0:T(8,128)} %convolution_bitcast_fusion.2) | data formatting | bytes 8388608 | tf_op jit(solution)/shard_map/pq,vqr->vpr/transpose | solution.py:72
  288.1 4.9 all-to-all-start.1
  293.4 47.0 %all-to-all-done.1 = f32[1,64,2,64,128]{4,3,2,0,1:T(8,128)} async-done(((f32[1,64,2,64,128]{4,3,2,0,1:T(8,128)}), f32[1,64,2,64,128]{4,3,2,0,1:T(8,128)}, u32[]{:S(2)}, u32[]{:S(2)}) %all-to-all-start.1) | async-done | bytes 4194336 | tf_op jit(solution)/shard_map/all_to_all | solution.py:121
  342.9 7.5 %multiply_reduce_fusion.1 = (f32[]{:T(128)}, f32[16,128,512]{2,1,0:T(8,128)S(1)}) fusion(f32[16,512,128]{2,1,0:T(8,128)S(1)} %bitcast.305, f32[256,512]{1,0:T(8,128)S(1)} %get-tuple-element.109, f32[256,512]{1,0:T(8,128)S(1)} %get-tuple-element.121), kind=kOutput, calls=%fused_computation.33 | convolution fusion | flops 6444810240 | bytes 9437188 | tf_op jit(solution)/shard_map/nq,vzqy->vzny/dot_general | solution.py:124
  358.9 8.1 %all-gather.2 = f32[4,1,5]{2,1,0:T(1,128)S(1)} all-gather(f32[1,1,5]{2,1,0:T(1,128)S(1)} %bitcast.329), channel_id=2, replica_groups=mesh['tm'=8,'space'=4] {'space'}, dimensions={0}, use_global_device_ids=true | all-gather | bytes 100 | tf_op jit(solution)/shard_map/all_gather | solution.py:152
  372.5 9.9 %multiply_subtract_fusion.3 = (f32[1,64,1,64,128]{4,2,1,3,0:T(1,128)S(1)}, f32[1,64,1,64,128]{4,2,1,3,0:T(1,128)S(1)}) fusion(f32[64,128]{1,0:T(8,128)S(1)} %get-tuple-element.114, f32[64]{0:T(128)S(1)} %multiply_sine_fusion.3, f32[64,128]{1,0:T(8,128)S(1)} %get-tuple-element.113, f32[64]{0:T(128)S(1)} %multiply_cosine_fusion.3, ...), kind=kLoop, calls=%fused_computation.60 | loop fusion | flops 6291456 | bytes 8454656 | tf_op jit(solution)/shard_map/sub | solution.py:163
  382.4 6.3 maximum_bitcast_fusion
  388.7 97.2 %all-reduce.5.cloned.1.call-done = (f32[64,2,64,128]{3,1,0,2:T(2,128)}, f32[64,2,128]{2,1,0:T(2,128)}) async-done(((f32[64,2,64,128]{3,1,0,2:T(2,128)}, f32[64,2,128]{2,1,0:T(2,128)}), (f32[64,2,64,128]{3,1,0,2:T(2,128)}, f32[64,2,128]{2,1,0:T(2,128)})) %all-reduce.5.cloned.1.call-update) | async-done | bytes 4259856 | tf_op jit(solution)/shard_map/psum | solution.py:198
  490.4 12.6 %fusion.199 = (f32[1,64,1,64,128]{4,2,1,3,0:T(1,128)S(1)}, f32[1,64,1,64,128]{4,2,1,3,0:T(1,128)S(1)}, f32[1,64,1,64,128]{4,2,1,3,0:T(1,128)S(1)}) fusion(f32[1,64,2,64,128]{4,2,1,3,0:T(2,128)S(1)} %multiply_bitcast_fusion, f32[1,64,2,64,128]{4,2,1,3,0:T(2,128)S(1)} %copy-done.1), kind=kLoop, calls=%fused_computation.344 | loop fusion | flops 5767168 | bytes 14680064 | tf_op jit(solution)/shard_map/div | solution.py:135
  503.0 7.3 fusion.198
  517.5 11.5 %convolution_bitcast_fusion.1 = f32[1,128,8192]{1,2,0:T(8,128)} fusion(f32[128,128]{1,0:T(8,128)S(1)} %reshape.1882, f32[16,8,64,128]{3,2,1,0:T(8,128)S(1)} %bitcast.302), kind=kOutput, calls=%fused_computation.1 | convolution fusion | flops 1610612736 | bytes 8454144 | tf_op jit(solution)/shard_map/pq,vqr->vpr/dot_general | solution.py:72
  529.0 10.0 %copy.240 = f32[1,128,8192]{2,0,1:T(1,128)} copy(f32[1,128,8192]{1,2,0:T(8,128)} %convolution_bitcast_fusion.1) | data formatting | bytes 8388608 | tf_op jit(solution)/shard_map/pq,vqr->vpr/transpose | solution.py:72
  550.4 51.2 %all_to_all.60 = f32[1,64,2,64,128]{4,3,2,0,1:T(8,128)S(1)} all-to-all(f32[1,64,2,64,128]{4,3,2,0,1:T(8,128)S(1)} %copy.243), channel_id=1, replica_groups=mesh['tm'=8,'space'=4] {'space'}, dimensions={1} | all-to-all | bytes 8388608 | tf_op jit(solution)/shard_map/all_to_all | solution.py:121
  602.1 7.5 %multiply_reduce_fusion = (f32[]{:T(128)}, f32[16,128,512]{2,1,0:T(8,128)S(1)}) fusion(f32[16,512,128]{2,1,0:T(8,128)S(1)} %bitcast.306, f32[256,512]{1,0:T(8,128)S(1)} %get-tuple-element.109, f32[256,512]{1,0:T(8,128)S(1)} %get-tuple-element.121), kind=kOutput, calls=%fused_computation.32 | convolution fusion | flops 6444810240 | bytes 9437188 | tf_op jit(solution)/shard_map/nq,vzqy->vzny/dot_general | solution.py:124
  618.1 7.4 all-gather.3
  630.0 10.1 %multiply_subtract_fusion = (f32[1,64,1,64,128]{4,2,1,3,0:T(1,128)S(1)}, f32[1,64,1,64,128]{4,2,1,3,0:T(1,128)S(1)}) fusion(f32[64,128]{1,0:T(8,128)S(1)} %get-tuple-element.112, f32[64]{0:T(128)S(1)} %multiply_sine_fusion.1, f32[64,128]{1,0:T(8,128)S(1)} %get-tuple-element.111, f32[64]{0:T(128)S(1)} %multiply_cosine_fusion.1, ...), kind=kLoop, calls=%fused_computation.51 | loop fusion | flops 6291456 | bytes 8454656 | tf_op jit(solution)/shard_map/sub | solution.py:163
  647.2 8.5 %convolution_bitcast_fusion = f32[1,128,8192]{1,2,0:T(8,128)} fusion(f32[128,128]{1,0:T(8,128)S(1)} %reshape.1882, f32[16,8,64,128]{3,2,1,0:T(8,128)S(1)} %bitcast.308), kind=kOutput, calls=%fused_computation | convolution fusion | flops 805306368 | bytes 8454144 | tf_op jit(solution)/shard_map/pq,vqr->vpr/dot_general | solution.py:72
  655.7 9.6 %copy.251 = f32[1,128,8192]{2,0,1:T(1,128)} copy(f32[1,128,8192]{1,2,0:T(8,128)} %convolution_bitcast_fusion) | data formatting | bytes 8388608 | tf_op jit(solution)/shard_map/pq,vqr->vpr/transpose | solution.py:72
  673.2 47.3 %all_to_all.61 = f32[1,64,2,64,128]{4,3,2,0,1:T(8,128)S(1)} all-to-all(f32[1,64,2,64,128]{4,3,2,0,1:T(8,128)S(1)} %copy.254), channel_id=1, replica_groups=mesh['tm'=8,'space'=4] {'space'}, dimensions={1} | all-to-all | bytes 8388608 | tf_op jit(solution)/shard_map/all_to_all | solution.py:121
  721.0 5.0 convolution_bitcast_fusion.4
  726.0 5.3 copy.257
  (136 shorter events, 128.7 us)
Async XLA Ops:
  33.6 53.8 %all-to-all-start = ((f32[1,16,2,256,128]{4,1,2,0,3:T(8,128)}), f32[1,16,2,256,128]{4,1,2,0,3:T(8,128)}, u32[]{:S(2)}, u32[]{:S(2)}) async-start(f32[1,16,2,256,128]{4,1,2,0,3:T(8,128)} %copy.208), calls=%async_computation | async-start | bytes 8388608 | tf_op jit(solution)/shard_map/all_to_all | solution.py:85
  38.8 183.5 %all-reduce.7.cloned.1.call-start = ((), (), s32[]{:S(2)}) async-start(), calls=%async_computation.5 | async-start | bytes 8519680 | tf_op jit(solution)/shard_map/psum | solution.py:198
  222.3 4.5 copy-start
  247.6 2.3 copy-start.5
  275.1 3.9 copy-start.2
  288.1 52.3 %all-to-all-start.1 = ((f32[1,64,2,64,128]{4,3,2,0,1:T(8,128)}), f32[1,64,2,64,128]{4,3,2,0,1:T(8,128)}, u32[]{:S(2)}, u32[]{:S(2)}) async-start(f32[1,64,2,64,128]{4,3,2,0,1:T(8,128)} %copy.232), calls=%async_computation.1 | async-start | bytes 8388608 | tf_op jit(solution)/shard_map/all_to_all | solution.py:121
  293.0 192.9 %all-reduce.5.cloned.1.call-start = ((), (), s32[]{:S(2)}) async-start(), calls=%async_computation.4 | async-start | bytes 8519680 | tf_op jit(solution)/shard_map/psum | solution.py:198
  485.9 4.5 copy-start.1
  510.4 4.2 copy-start.6
  539.0 3.9 copy-start.3
  627.0 13.1 %copy-start.7 = (f32[1,3]{1,0:T(1,128)}, f32[1,3]{1,0:T(1,128)S(1)}, u32[]{:S(2)}) copy-start(f32[1,3]{1,0:T(1,128)S(1)} %slice_divide_fusion) | copy-start | bytes 40
  665.3 3.0 copy-start.4
Sparse Core Ops, SparseCore 0:
  124.0 98.2 all-reduce.6
  388.8 97.0 all-reduce.4
